TPU v7x, 256 devices: a whole 4x4x8 slice. The times are simulated.
256 devices in a mesh: view: 8 (over x, y_lo), tile: 32 (over z, y_hi, core).
Axes of the slice: x: 4, y: 4 (y_hi: 2, y_lo: 2; y = y_hi * 2 + y_lo), z: 8, core: 2. Of those that a mesh axis runs over, the one named last changes fastest.
Arguments:
- latents: bfloat16 [16, 2048, 1536], P('view', 'tile'), may hold values from -14 to 14
- qkv_weight: bfloat16 [1536, 3072], replicated, may hold values from -0.15625 to 0.15625
- out_weight: bfloat16 [1024, 1536], replicated, may hold values from -0.1875 to 0.1875
- anchor: int32 [1], replicated, may hold values from 0 to 15
- epi_list: int32 [16, 16, 6], P('view'), may hold values from -1 to 31, as said below
Outputs:
- attn_out: bfloat16 [16, 2048, 1536], P('view', 'tile')
Inputs may be any that keep to these rules, and one draw needn't show every extreme that they name: `epi_list`: row (v, b) lists distinct key blocks: an id c < 16 is block c of view (v - 1) mod 16, an id c >= 16 is block c - 16 of view (v + 1) mod 16; unused slots hold -1 and follow the used ones. Every row uses 1 to 6 slots, with a cap that varies from view to view, and some row uses all 6.
All inputs are finite; a program needn't handle non-finite values.
Results may differ from a plain program's by a relative error of at most 0.005.
The roundings to bfloat16 on the way count: a program that leaves them out, or rounds other values in their place, can miss the bound.
Values may be sent and summed in bfloat16 or wider, within the bound.
No kernel may reach another device: no remote copies, remote signals or barrier semaphores. Data moves between devices by JAX's collectives and lax.ppermute only.
A program may use at most 128 MiB of HBM per device.

v0:
```python
import math
import jax
import jax.numpy as jnp
from jax import lax
from jax.sharding import PartitionSpec as P

HEADS = 8
HD = 128
VT = 2048
BLK = 128
NBLK = 16


def spread_2(array, axis, root):
    mine = lax.axis_index(axis) == root
    return lax.psum(jnp.where(mine, array, jnp.zeros_like(array)), axis)


def from_behind(array, axis, by):
    count = lax.axis_size(axis)
    return lax.ppermute(array, axis, [(i, (i + by) % count) for i in range(count)])


def allowed_tokens(epi_rows):
    blocks = jnp.any(
        epi_rows[:, :, None] == jnp.arange(2 * NBLK, dtype=jnp.int32)[None, None, :], axis=1
    )
    nearby = jnp.repeat(jnp.repeat(blocks, BLK, axis=0), BLK, axis=1)
    always = jnp.ones((VT, VT), dtype=bool)
    return jnp.concatenate([always, nearby, always], axis=1)


def attend(queries, keys_part, values_part, allowed):
    scores = jnp.einsum(
        "qd,kd->qk", queries, keys_part, preferred_element_type=jnp.float32
    ) / math.sqrt(HD)
    scores = jnp.where(allowed, scores, -jnp.inf)
    row_peak = jnp.max(scores, axis=1, keepdims=True)
    raised = jnp.exp(scores - row_peak)
    row_total = jnp.sum(raised, axis=1, keepdims=True)
    weights = raised.astype(jnp.bfloat16)
    summed = jnp.einsum("qk,kd->qd", weights, values_part, preferred_element_type=jnp.float32)
    return (summed / row_total).astype(jnp.bfloat16)


def body(latents, qkv_weight, out_weight, anchor, epi_list):
    per_dev, tile_tokens, model_width = latents.shape
    tile_count = lax.axis_size("tile")
    view_tokens = tile_tokens * tile_count
    parts = max(1, tile_count // (per_dev * HEADS))
    units = per_dev * HEADS * parts // tile_count
    part_rows = view_tokens // parts
    per_view = tile_count // per_dev
    shaped = qkv_weight.reshape(model_width, HEADS, 3 * HD)
    projected = jnp.einsum(
        "vtd,dhc->vhtc", latents, shaped, preferred_element_type=jnp.float32
    ).astype(jnp.bfloat16)
    key_values = projected[..., HD:]

    def spread(source):
        wide = jnp.broadcast_to(source[:, :, None], (per_dev, HEADS, parts) + source.shape[2:])
        return wide.reshape(tile_count, units, tile_tokens, source.shape[-1])

    target = anchor[0]
    anchor_tile = lax.dynamic_index_in_dim(key_values, target % per_dev, 0, keepdims=False)
    anchor_tile = spread_2(anchor_tile, "view", target // per_dev)
    anchor_send = spread(jnp.broadcast_to(anchor_tile[None], key_values.shape))
    boundary = [
        from_behind(key_values[per_dev - 1 if offset == 1 else 0], "view", offset)
        for offset in (1, -1)
    ]
    earlier = jnp.concatenate([boundary[0][None], key_values[:-1]], axis=0)
    following = jnp.concatenate([key_values[1:], boundary[1][None]], axis=0)
    resident, anchored, earlier, following = (
        lax.all_to_all(spread(projected), "tile", split_axis=0, concat_axis=2, tiled=True),
        lax.all_to_all(anchor_send, "tile", split_axis=0, concat_axis=2, tiled=True),
        lax.all_to_all(spread(earlier), "tile", split_axis=0, concat_axis=2, tiled=True),
        lax.all_to_all(spread(following), "tile", split_axis=0, concat_axis=2, tiled=True),
    )
    resident, anchored, earlier, following = (resident[0], anchored[0], earlier[0], following[0])
    tile_index = lax.axis_index("tile")
    local_view = tile_index // per_view
    epi_rows = lax.dynamic_index_in_dim(epi_list, local_view, 0, keepdims=False)
    allowed = allowed_tokens(epi_rows)
    joined = jnp.concatenate([resident[..., HD:], earlier, following, anchored], axis=1)
    block_rows = min(512, part_rows)
    block_count = part_rows // block_rows
    part_ids = (tile_index * units + jnp.arange(units, dtype=jnp.int32)) % parts

    def one_unit(unit_items):
        all_queries, keyvals, part_id = unit_items
        start = part_id * part_rows
        queries = lax.dynamic_slice_in_dim(all_queries, start, part_rows, 0).reshape(
            block_count, block_rows, HD
        )
        mask_rows = lax.dynamic_slice_in_dim(allowed, start, part_rows, 0).reshape(
            block_count, block_rows, 4 * view_tokens
        )

        def one_block(block_items):
            query_rows, block_mask = block_items
            return attend(query_rows, keyvals[:, :HD], keyvals[:, HD:], block_mask)

        return lax.map(one_block, (queries, mask_rows)).reshape(part_rows, HD)

    attended = lax.map(one_unit, (resident[..., :HD], joined, part_ids))
    pieces = attended.reshape(units, tile_count // parts, tile_tokens, HD).transpose(1, 0, 2, 3)
    selected = part_ids[None, :] == jnp.arange(parts, dtype=jnp.int32)[:, None]
    outgoing = jnp.where(
        selected[:, None, :, None, None], pieces[None], jnp.zeros((), jnp.bfloat16)
    )
    outgoing = outgoing.reshape(tile_count, units, tile_tokens, HD)
    returned = lax.all_to_all(outgoing, "tile", split_axis=0, concat_axis=1, tiled=True).reshape(
        per_dev, HEADS, parts, tile_tokens, HD
    )
    own_part = tile_index // (tile_count // parts)
    returned = lax.dynamic_index_in_dim(returned, own_part, 2, keepdims=False)
    projected_out = jnp.einsum(
        "vhtc,hcd->vtd",
        returned,
        out_weight.reshape(HEADS, HD, model_width),
        preferred_element_type=jnp.float32,
    )
    return projected_out.astype(jnp.bfloat16)


def solution(mesh):
    return jax.shard_map(
        body,
        mesh=mesh,
        in_specs=(P("view", "tile", None), P(), P(), P(), P("view", None, None)),
        out_specs=P("view", "tile", None),
        check_vma=False,
    )
```

profile of v0, /device:TPU:1, one launch (start us, length us, event | category | flops | bytes accessed | tf_op | source)
XLA Modules:
  0.0 359.8 jit_solution(12178638410884867979)
XLA Ops:
  7.4 9.8 %copy.35 = bf16[192,8,8,384]{3,2,1,0:T(8,128)(2,1)} copy(bf16[192,8,8,384]{3,1,2,0:T(8,128)(2,1)} %bitcast.80) | data formatting | bytes 18874368
  17.1 5.1 %fusion.38 = bf16[2,8,64,384]{3,2,0,1:T(8,128)(2,1)S(1)} fusion(bf16[1536,8,384,1]{2,1,0,3:T(8,128)(2,1)} %bitcast.81, bf16[2,64,1536]{2,1,0:T(8,128)(2,1)S(1)} %copy-done.3), kind=kOutput, calls=%fused_computation.27 | convolution fusion | flops 1208352768 | bytes 10616832 | tf_op jit(solution)/shard_map/vtd,dhc->vhtc/dot_general | solution.py:55
  25.7 78.0 %all-reduce.2.cloned.1.call-done = bf16[8,64,256]{2,1,0:T(8,128)(2,1)} async-done(((bf16[8,64,256]{2,1,0:T(8,128)(2,1)}), bf16[8,64,256]{2,1,0:T(8,128)(2,1)}) %all-reduce.2.cloned.1.call-update) | async-done | bytes 262160 | tf_op jit(solution)/shard_map/psum | solution.py:16
  105.7 15.3 %all-to-all-start.3 = ((bf16[32,1,64,256]{3,2,1,0:T(8,128)(2,1)}), bf16[32,1,64,256]{3,2,1,0:T(8,128)(2,1)}, u32[]{:S(2)}, u32[]{:S(2)}) async-start(bf16[32,1,64,256]{3,2,1,0:T(8,128)(2,1)} %bitcast.83), calls=%async_computation.3 | async-start | bytes 2097152 | tf_op jit(solution)/shard_map/all_to_all | solution.py:76
  123.8 10.8 %collective-permute-done = bf16[8,64,256]{2,1,0:T(8,128)(2,1)S(1)} collective-permute-done((bf16[8,64,256]{2,1,0:T(8,128)(2,1)S(1)}, bf16[8,64,256]{2,1,0:T(8,128)(2,1)S(1)}, u32[]{:S(2)}, u32[]{:S(2)}) %collective-permute-start) | collective-permute-done | bytes 262176 | tf_op jit(solution)/shard_map/ppermute | solution.py:21
  135.5 13.6 %all-to-all-done.3 = bf16[32,1,64,256]{3,2,1,0:T(8,128)(2,1)} async-done(((bf16[32,1,64,256]{3,2,1,0:T(8,128)(2,1)}), bf16[32,1,64,256]{3,2,1,0:T(8,128)(2,1)}, u32[]{:S(2)}, u32[]{:S(2)}) %all-to-all-start.3) | async-done | bytes 1048608 | tf_op jit(solution)/shard_map/all_to_all | solution.py:76
  151.2 5.9 %all-to-all-start.1 = ((bf16[32,1,64,256]{3,2,1,0:T(8,128)(2,1)}), bf16[32,1,64,256]{3,2,1,0:T(8,128)(2,1)}, u32[]{:S(2)}, u32[]{:S(2)}) async-start(bf16[32,1,64,256]{3,2,1,0:T(8,128)(2,1)} %bitcast.85), calls=%async_computation.1 | async-start | bytes 2097152 | tf_op jit(solution)/shard_map/all_to_all | solution.py:77
  159.2 26.0 %all-to-all-done.1 = bf16[32,1,64,256]{3,2,1,0:T(8,128)(2,1)} async-done(((bf16[32,1,64,256]{3,2,1,0:T(8,128)(2,1)}), bf16[32,1,64,256]{3,2,1,0:T(8,128)(2,1)}, u32[]{:S(2)}, u32[]{:S(2)}) %all-to-all-start.1) | async-done | bytes 1048608 | tf_op jit(solution)/shard_map/all_to_all | solution.py:77
  187.8 5.9 %all-to-all-start = ((bf16[32,1,64,384]{3,2,1,0:T(8,128)(2,1)}), bf16[32,1,64,384]{3,2,1,0:T(8,128)(2,1)}, u32[]{:S(2)}, u32[]{:S(2)}) async-start(bf16[32,1,64,384]{3,2,1,0:T(8,128)(2,1)} %bitcast.82), calls=%async_computation | async-start | bytes 3145728 | tf_op jit(solution)/shard_map/all_to_all | solution.py:75
  195.2 11.2 %broadcast_in_dim.89 = pred[2048,32,128]{2,1,0:T(8,128)(4,1)S(1)} broadcast(pred[2048,32]{1,0:T(8,128)(4,1)S(1)} %bitcast.89), dimensions={0,1} | broadcast | bytes 8454144 | tf_op jit(solution)/shard_map/broadcast_in_dim | solution.py:28
  206.5 7.9 %copy.46 = pred[256,8,32,128]{3,1,2,0:T(8,128)(4,1)} copy(pred[256,8,32,128]{3,2,1,0:T(8,128)(4,1)S(1)} %bitcast.79) | data formatting | bytes 16777216
  216.4 16.6 %all-to-all-done = bf16[32,1,64,384]{3,2,1,0:T(8,128)(2,1)} async-done(((bf16[32,1,64,384]{3,2,1,0:T(8,128)(2,1)}), bf16[32,1,64,384]{3,2,1,0:T(8,128)(2,1)}, u32[]{:S(2)}, u32[]{:S(2)}) %all-to-all-start) | async-done | bytes 1572896 | tf_op jit(solution)/shard_map/all_to_all | solution.py:75
  235.1 6.3 %all-to-all-start.2 = ((bf16[32,1,64,256]{3,2,1,0:T(8,128)(2,1)}), bf16[32,1,64,256]{3,2,1,0:T(8,128)(2,1)}, u32[]{:S(2)}, u32[]{:S(2)}) async-start(bf16[32,1,64,256]{3,2,1,0:T(8,128)(2,1)} %bitcast.84), calls=%async_computation.2 | async-start | bytes 2097152 | tf_op jit(solution)/shard_map/all_to_all | solution.py:78
  242.5 7.9 %fusion.31 = pred[1024,8192]{1,0:T(32,128)(4,1)} fusion(s32[]{:T(128)S(6)} %select_n.67, pred[2048,2048]{1,0:T(32,128)(4,1)S(1)} %broadcast_in_dim.87, pred[2048,4096]{1,0:T(8,128)(4,1)} %bitcast.78), kind=kLoop, calls=%fused_computation.19 | loop fusion | flops 16777216 | bytes 20971524 | tf_op jit(solution)/shard_map/concatenate | solution.py:30
  253.8 15.5 %all-to-all-done.2 = bf16[32,1,64,256]{3,2,1,0:T(8,128)(2,1)} async-done(((bf16[32,1,64,256]{3,2,1,0:T(8,128)(2,1)}), bf16[32,1,64,256]{3,2,1,0:T(8,128)(2,1)}, u32[]{:S(2)}, u32[]{:S(2)}) %all-to-all-start.2) | async-done | bytes 1048608 | tf_op jit(solution)/shard_map/all_to_all | solution.py:78
  269.3 3.8 %maximum_bitcast_fusion = bf16[8192,256]{1,0:T(8,128)(2,1)} fusion(bf16[1,2048,256]{2,1,0:T(8,128)(2,1)} %bitcast.26, bf16[1,2048,256]{2,1,0:T(8,128)(2,1)} %bitcast.22, bf16[1,2048,256]{2,1,0:T(8,128)(2,1)} %bitcast.18, bf16[1,2048,256]{2,1,0:T(8,128)(2,1)} %slice.31), kind=kLoop, calls=%fused_computation.23 | loop fusion | flops 16777216 | bytes 8388608 | tf_op jit(solution)/shard_map/while/body/jit(dynamic_index_in_dim)/squeeze | solution.py:106
  273.1 54.6 %while.17 = (s32[]{:T(128)}, bf16[2,512,128]{2,1,0:T(8,128)(2,1)}, pred[2,512,8192]{2,1,0:T(32,128)(4,1)}, bf16[2,512,128]{2,1,0:T(8,128)(2,1)S(1)}, bf16[8192,256]{1,0:T(8,128)(2,1)}, /*index=5*/s32[]{:T(128)}) while((s32[]{:T(128)}, bf16[2,512,128]{2,1,0:T(8,128)(2,1)}, pred[2,512,8192]{2,1,0:T(32,128)(4,1)}, ...), condition=%wide.region_5.6_spmd, body=%wide.region_2.5_spmd.sunk | while | flops 2176973824 | bytes 58994244 | solution.py:104
  273.1 9.8 %fusion.56 = (f32[512]{0:T(512)S(1)}, f32[512,8192]{1,0:T(8,128)}) fusion(bf16[8192,256]{1,0:T(8,128)(2,1)} %get-tuple-element.118, bf16[2,512,128]{2,1,0:T(8,128)(2,1)S(1)} %get-tuple-element.117, s32[]{:T(128)} %get-tuple-element.108, pred[2,512,8192]{2,1,0:T(32,128)(4,1)} %get-tuple-element.116), kind=kOutput, calls=%fused_computation.45.clone.1 | convolution fusion | flops 1086324224 | bytes 23202816 | tf_op jit(solution)/shard_map/while/body/eval_jaxpr/while/body/eval_jaxpr/qd,kd->qk/dot_general | solution.py:34
  282.9 8.1 %fusion.57 = f32[512]{0:T(512)S(1)} fusion(f32[512,8192]{1,0:T(8,128)} %get-tuple-element.100, f32[512]{0:T(512)S(1)} %get-tuple-element.101), kind=kLoop, calls=%fused_computation.2.clone.1 | loop fusion | flops 8388096 | bytes 16781312 | tf_op jit(solution)/shard_map/while/body/eval_jaxpr/while/body/eval_jaxpr/reduce_sum | solution.py:40
  291.0 9.4 %fusion.58 = bf16[2,512,128]{2,1,0:T(8,128)(2,1)} fusion(bf16[2,512,128]{2,1,0:T(8,128)(2,1)} %get-tuple-element.109, s32[]{:T(128)} %get-tuple-element.108, bf16[8192,256]{1,0:T(8,128)(2,1)} %get-tuple-element.118, f32[512,8192]{1,0:T(8,128)} %get-tuple-element.100, f32[512]{0:T(512)S(1)} %get-tuple-element.101, f32[512]{0:T(512)S(1)} %fusion.57), kind=kOutput, calls=%fused_computation.11.clone.1 | convolution fusion | flops 1082261504 | bytes 19010048 | tf_op jit(solution)/shard_map/while/body/eval_jaxpr/while/body/eval_jaxpr/qk,kd->qd/dot_general | solution.py:42
  300.4 9.8 %fusion.56 = (f32[512]{0:T(512)S(1)}, f32[512,8192]{1,0:T(8,128)}) fusion(bf16[8192,256]{1,0:T(8,128)(2,1)} %get-tuple-element.118, bf16[2,512,128]{2,1,0:T(8,128)(2,1)S(1)} %get-tuple-element.117, s32[]{:T(128)} %get-tuple-element.108, pred[2,512,8192]{2,1,0:T(32,128)(4,1)} %get-tuple-element.116), kind=kOutput, calls=%fused_computation.45.clone.1 | convolution fusion | flops 1086324224 | bytes 23202816 | tf_op jit(solution)/shard_map/while/body/eval_jaxpr/while/body/eval_jaxpr/qd,kd->qk/dot_general | solution.py:34
  310.2 8.1 %fusion.57 = f32[512]{0:T(512)S(1)} fusion(f32[512,8192]{1,0:T(8,128)} %get-tuple-element.100, f32[512]{0:T(512)S(1)} %get-tuple-element.101), kind=kLoop, calls=%fused_computation.2.clone.1 | loop fusion | flops 8388096 | bytes 16781312 | tf_op jit(solution)/shard_map/while/body/eval_jaxpr/while/body/eval_jaxpr/reduce_sum | solution.py:40
  318.3 9.4 %fusion.58 = bf16[2,512,128]{2,1,0:T(8,128)(2,1)} fusion(bf16[2,512,128]{2,1,0:T(8,128)(2,1)} %get-tuple-element.109, s32[]{:T(128)} %get-tuple-element.108, bf16[8192,256]{1,0:T(8,128)(2,1)} %get-tuple-element.118, f32[512,8192]{1,0:T(8,128)} %get-tuple-element.100, f32[512]{0:T(512)S(1)} %get-tuple-element.101, f32[512]{0:T(512)S(1)} %fusion.57), kind=kOutput, calls=%fused_computation.11.clone.1 | convolution fusion | flops 1082261504 | bytes 19010048 | tf_op jit(solution)/shard_map/while/body/eval_jaxpr/while/body/eval_jaxpr/qk,kd->qd/dot_general | solution.py:42
  328.9 22.7 %all_to_all.20 = bf16[32,1,64,128]{3,2,1,0:T(8,128)(2,1)S(1)} all-to-all(bf16[32,1,64,128]{3,2,1,0:T(8,128)(2,1)S(1)} %broadcast_select_fusion), channel_id=1, replica_groups=mesh['view'=8,'tile'=32] {'tile'}, dimensions={0} | all-to-all | bytes 1048576 | tf_op jit(solution)/shard_map/all_to_all | solution.py:113
  (39 shorter events, 28.5 us)
Async XLA Ops:
  6.5 345.1 %copy-start = (bf16[1024,1536]{1,0:T(8,128)(2,1)S(1)}, bf16[1024,1536]{1,0:T(8,128)(2,1)}, u32[]{:S(2)}) copy-start(bf16[1024,1536]{1,0:T(8,128)(2,1)} %param.9) | copy-start | bytes 9437188
  6.5 97.1 %all-reduce.2.cloned.1.call-start = ((), (), s32[]{:S(2)}) async-start(), calls=%async_computation.5 | async-start | bytes 524288 | tf_op jit(solution)/shard_map/psum | solution.py:16
  7.4 9.8 %copy-start.3 = (bf16[2,64,1536]{2,1,0:T(8,128)(2,1)S(1)}, bf16[2,64,1536]{2,1,0:T(8,128)(2,1)}, u32[]{:S(2)}) copy-start(bf16[2,64,1536]{2,1,0:T(8,128)(2,1)} %param.7) | copy-start | bytes 1179652
  22.2 0.9 copy-start.1
  25.7 169.3 %copy-start.2 = (s32[2,16,6]{1,0,2:T(2,128)S(1)}, s32[2,16,6]{1,0,2:T(2,128)}, u32[]{:S(2)}) copy-start(s32[2,16,6]{1,0,2:T(2,128)} %param.11) | copy-start | bytes 2308
  105.7 43.4 %all-to-all-start.3 = ((bf16[32,1,64,256]{3,2,1,0:T(8,128)(2,1)}), bf16[32,1,64,256]{3,2,1,0:T(8,128)(2,1)}, u32[]{:S(2)}, u32[]{:S(2)}) async-start(bf16[32,1,64,256]{3,2,1,0:T(8,128)(2,1)} %bitcast.83), calls=%async_computation.3 | async-start | bytes 2097152 | tf_op jit(solution)/shard_map/all_to_all | solution.py:76
  122.0 12.6 %collective-permute-start = (bf16[8,64,256]{2,1,0:T(8,128)(2,1)S(1)}, bf16[8,64,256]{2,1,0:T(8,128)(2,1)S(1)}, u32[]{:S(2)}, u32[]{:S(2)}) collective-permute-start(bf16[8,64,256]{2,1,0:T(8,128)(2,1)S(1)} %get-tuple-element.63), channel_id=1, source_target_pairs={{0,32},{32,64},{64,96},{96,128},{128,160},{160,192},{192,224},{224... | collective-permute-start | bytes 786440 | tf_op jit(solution)/shard_map/ppermute | solution.py:21
  151.2 34.0 %all-to-all-start.1 = ((bf16[32,1,64,256]{3,2,1,0:T(8,128)(2,1)}), bf16[32,1,64,256]{3,2,1,0:T(8,128)(2,1)}, u32[]{:S(2)}, u32[]{:S(2)}) async-start(bf16[32,1,64,256]{3,2,1,0:T(8,128)(2,1)} %bitcast.85), calls=%async_computation.1 | async-start | bytes 2097152 | tf_op jit(solution)/shard_map/all_to_all | solution.py:77
  187.8 45.2 %all-to-all-start = ((bf16[32,1,64,384]{3,2,1,0:T(8,128)(2,1)}), bf16[32,1,64,384]{3,2,1,0:T(8,128)(2,1)}, u32[]{:S(2)}, u32[]{:S(2)}) async-start(bf16[32,1,64,384]{3,2,1,0:T(8,128)(2,1)} %bitcast.82), calls=%async_computation | async-start | bytes 3145728 | tf_op jit(solution)/shard_map/all_to_all | solution.py:75
  193.6 20.9 %collective-permute-start.1 = (bf16[8,64,256]{2,1,0:T(8,128)(2,1)}, bf16[8,64,256]{2,1,0:T(8,128)(2,1)}, u32[]{:S(2)}, u32[]{:S(2)}) collective-permute-start(bf16[8,64,256]{2,1,0:T(8,128)(2,1)} %get-tuple-element.66), channel_id=1, source_target_pairs={{0,224},{32,0},{64,32},{96,64},{128,96},{160,128},{192,160},{224,1... | collective-permute-start | bytes 786440 | tf_op jit(solution)/shard_map/ppermute | solution.py:21
  235.1 34.2 %all-to-all-start.2 = ((bf16[32,1,64,256]{3,2,1,0:T(8,128)(2,1)}), bf16[32,1,64,256]{3,2,1,0:T(8,128)(2,1)}, u32[]{:S(2)}, u32[]{:S(2)}) async-start(bf16[32,1,64,256]{3,2,1,0:T(8,128)(2,1)} %bitcast.84), calls=%async_computation.2 | async-start | bytes 2097152 | tf_op jit(solution)/shard_map/all_to_all | solution.py:78
Sparse Core Ops, SparseCore 0:
  25.8 77.8 all-reduce.1
where the time goes:
time: 361 us; the launch traced here: 360 us
  waiting for transfers between devices  161 us (45%)
  local copies, waits for them, and re-layouts  50 us (14%)
  matrix products  44.8 us (12%)
  starting transfers between devices  34.8 us (10%)
  other arithmetic  32.4 us (9%)
  blocking collectives  22.7 us (6%)
  between operations  14.4 us (4%)
    psum x1, waiting for transfers between devices, spread_2(): return lax.psum(jnp.where(mine, array, jnp.zeros_like(array)), axis)  78 us
    all_to_all x1, waiting for transfers between devices, body(): lax.all_to_all(spread(earlier), 'tile', split_axis=0, concat_axis=2, tile...  26 us
    all_to_all x1, blocking collectives, body(): lax.all_to_all(outgoing, 'tile', split_axis=0, concat_axis=1, tiled=True)  22.7 us
    dot_general x2, matrix products, attend(): jnp.einsum('qd,kd->qk', queries, keys_part, preferred_element_type=jnp.fl...  19.6 us
    dot_general x2, matrix products, attend(): jnp.einsum('qk,kd->qd', weights, values_part, preferred_element_type=jnp....  18.8 us
    unnamed x11, local copies, waits for them, and re-layouts  18.6 us
    all_to_all x1, waiting for transfers between devices, body(): lax.all_to_all(spread(projected), 'tile', split_axis=0, concat_axis=2, ti...  16.6 us
    reduce_sum x2, other arithmetic, attend(): row_total = jnp.sum(raised, axis=1, keepdims=True)  16.2 us
  transfers between devices with their start and end apart: 7, of which 6 were waited for; matrix products, arithmetic and copies ran while one was open for 11% of the time, Pallas kernels for 0%

commit v1 on v0

--- a/solution.py
+++ b/solution.py
@@ -13,7 +13,7 @@
 
 def spread_2(array, axis, root):
     mine = lax.axis_index(axis) == root
-    return lax.psum(jnp.where(mine, array, jnp.zeros_like(array)), axis)
+    return jnp.sum(lax.all_gather(jnp.where(mine, array, jnp.zeros_like(array)), axis), axis=0)
 
 
 def from_behind(array, axis, by):

time: 361 us -> 297 us (0.82)
  waiting for transfers between devices: 161 us -> 93.2 us
  starting transfers between devices: 34.8 us -> 41.6 us
    psum x1 -> x0, waiting for transfers between devices: 78 us -> none  [spread_2(): return lax.psum(jnp.where(mine, array, jnp.zeros_like(array)), axis)]
    all_gather x0 -> x1, waiting for transfers between devices: none -> 24 us  [spread_2(): lax.all_gather(jnp.where(mine, array, jnp.zeros_like(array)), axis)]
    all_to_all x1, waiting for transfers between devices: 16.6 us -> 0.01 us  [body(): lax.all_to_all(spread(projected), 'tile', split_axis=0, concat_axis=2, ti...]
    all_to_all x1, waiting for transfers between devices: 26 us -> 14.5 us  [body(): lax.all_to_all(spread(earlier), 'tile', split_axis=0, concat_axis=2, tile...]
    all_to_all x1, starting transfers between devices: 5.88 us -> 14.9 us  [body(): lax.all_to_all(spread(earlier), 'tile', split_axis=0, concat_axis=2, tile...]
    ppermute x2, waiting for transfers between devices: 10.9 us -> 17.4 us  [from_behind(): lax.ppermute(array, axis, [(i, (i + by) % count) for i in range(count)])]
    all_to_all x1, waiting for transfers between devices: 15.5 us -> 21.7 us  [body(): lax.all_to_all(spread(following), 'tile', split_axis=0, concat_axis=2, ti...]
  transfers between devices with their start and end apart: 7 -> 7, of which waited for: 6 -> 6; matrix products, arithmetic and copies ran while one was open for 11% -> 15% of each run, Pallas kernels for 0% -> 0%
where the time goes in v1:
time: 297 us; the launch traced here: 296 us
  waiting for transfers between devices  93.2 us (31%)
  local copies, waits for them, and re-layouts  46.5 us (16%)
  matrix products  44.8 us (15%)
  starting transfers between devices  41.6 us (14%)
  other arithmetic  32.6 us (11%)
  blocking collectives  22.7 us (8%)
  between operations  14.3 us (5%)
    all_gather x1, waiting for transfers between devices, spread_2(): lax.all_gather(jnp.where(mine, array, jnp.zeros_like(array)), axis)  24 us
    all_to_all x1, blocking collectives, body(): lax.all_to_all(outgoing, 'tile', split_axis=0, concat_axis=1, tiled=True)  22.7 us
    all_to_all x1, waiting for transfers between devices, body(): lax.all_to_all(spread(following), 'tile', split_axis=0, concat_axis=2, ti...  21.7 us
    dot_general x2, matrix products, attend(): jnp.einsum('qd,kd->qk', queries, keys_part, preferred_element_type=jnp.fl...  19.6 us
    dot_general x2, matrix products, attend(): jnp.einsum('qk,kd->qd', weights, values_part, preferred_element_type=jnp....  18.8 us
    unnamed x11, local copies, waits for them, and re-layouts  17.7 us
    ppermute x2, waiting for transfers between devices, from_behind(): lax.ppermute(array, axis, [(i, (i + by) % count) for i in range(count)])  17.4 us
    reduce_sum x2, other arithmetic, attend(): row_total = jnp.sum(raised, axis=1, keepdims=True)  16.2 us
  transfers between devices with their start and end apart: 7, of which 6 were waited for; matrix products, arithmetic and copies ran while one was open for 15% of the time, Pallas kernels for 0%

profile of v1, /device:TPU:1, one launch (start us, length us, event | category | flops | bytes accessed | tf_op | source)
XLA Modules:
  0.0 295.7 jit_solution(9167689913716869115)
XLA Ops:
  6.5 9.8 %copy.35 = bf16[192,8,8,384]{3,2,1,0:T(8,128)(2,1)} copy(bf16[192,8,8,384]{3,1,2,0:T(8,128)(2,1)} %bitcast.78) | data formatting | bytes 18874368
  16.3 5.1 %fusion.38 = bf16[2,8,64,384]{3,2,0,1:T(8,128)(2,1)S(1)} fusion(bf16[1536,8,384,1]{2,1,0,3:T(8,128)(2,1)} %bitcast.79, bf16[2,64,1536]{2,1,0:T(8,128)(2,1)S(1)} %copy-done.3), kind=kOutput, calls=%fused_computation.27 | convolution fusion | flops 1208352768 | bytes 10616832 | tf_op jit(solution)/shard_map/vtd,dhc->vhtc/dot_general | solution.py:55
  24.4 5.2 %collective-permute-done = bf16[8,64,256]{2,1,0:T(8,128)(2,1)S(1)} collective-permute-done((bf16[8,64,256]{2,1,0:T(8,128)(2,1)S(1)}, bf16[8,64,256]{2,1,0:T(8,128)(2,1)S(1)}, u32[]{:S(2)}, u32[]{:S(2)}) %collective-permute-start) | collective-permute-done | bytes 262176 | tf_op jit(solution)/shard_map/ppermute | solution.py:21
  30.8 14.9 %all-to-all-start.1 = ((bf16[32,1,64,256]{3,2,1,0:T(8,128)(2,1)}), bf16[32,1,64,256]{3,2,1,0:T(8,128)(2,1)}, u32[]{:S(2)}, u32[]{:S(2)}) async-start(bf16[32,1,64,256]{3,2,1,0:T(8,128)(2,1)} %bitcast.83), calls=%async_computation.1 | async-start | bytes 2097152 | tf_op jit(solution)/shard_map/all_to_all | solution.py:77
  46.2 12.2 %collective-permute-done.1 = bf16[8,64,256]{2,1,0:T(8,128)(2,1)S(1)} collective-permute-done((bf16[8,64,256]{2,1,0:T(8,128)(2,1)}, bf16[8,64,256]{2,1,0:T(8,128)(2,1)S(1)}, u32[]{:S(2)}, u32[]{:S(2)}) %collective-permute-start.1) | collective-permute-done | bytes 262176 | tf_op jit(solution)/shard_map/ppermute | solution.py:21
  59.3 14.5 %all-to-all-done.1 = bf16[32,1,64,256]{3,2,1,0:T(8,128)(2,1)} async-done(((bf16[32,1,64,256]{3,2,1,0:T(8,128)(2,1)}), bf16[32,1,64,256]{3,2,1,0:T(8,128)(2,1)}, u32[]{:S(2)}, u32[]{:S(2)}) %all-to-all-start.1) | async-done | bytes 1048608 | tf_op jit(solution)/shard_map/all_to_all | solution.py:77
  75.9 5.9 %all-to-all-start.2 = ((bf16[32,1,64,256]{3,2,1,0:T(8,128)(2,1)}), bf16[32,1,64,256]{3,2,1,0:T(8,128)(2,1)}, u32[]{:S(2)}, u32[]{:S(2)}) async-start(bf16[32,1,64,256]{3,2,1,0:T(8,128)(2,1)} %bitcast.82), calls=%async_computation.2 | async-start | bytes 2097152 | tf_op jit(solution)/shard_map/all_to_all | solution.py:78
  88.3 21.7 %all-to-all-done.2 = bf16[32,1,64,256]{3,2,1,0:T(8,128)(2,1)} async-done(((bf16[32,1,64,256]{3,2,1,0:T(8,128)(2,1)}), bf16[32,1,64,256]{3,2,1,0:T(8,128)(2,1)}, u32[]{:S(2)}, u32[]{:S(2)}) %all-to-all-start.2) | async-done | bytes 1048608 | tf_op jit(solution)/shard_map/all_to_all | solution.py:78
  112.6 5.9 %all-to-all-start = ((bf16[32,1,64,384]{3,2,1,0:T(8,128)(2,1)}), bf16[32,1,64,384]{3,2,1,0:T(8,128)(2,1)}, u32[]{:S(2)}, u32[]{:S(2)}) async-start(bf16[32,1,64,384]{3,2,1,0:T(8,128)(2,1)} %bitcast.80), calls=%async_computation | async-start | bytes 3145728 | tf_op jit(solution)/shard_map/all_to_all | solution.py:75
  118.8 11.2 %broadcast_in_dim.89 = pred[2048,32,128]{2,1,0:T(8,128)(4,1)S(1)} broadcast(pred[2048,32]{1,0:T(8,128)(4,1)S(1)} %bitcast.87), dimensions={0,1} | broadcast | bytes 8454144 | tf_op jit(solution)/shard_map/broadcast_in_dim | solution.py:28
  130.0 7.9 %copy.46 = pred[256,8,32,128]{3,1,2,0:T(8,128)(4,1)} copy(pred[256,8,32,128]{3,2,1,0:T(8,128)(4,1)S(1)} %bitcast.77) | data formatting | bytes 16777216
  138.1 24.0 %all-gather.2.cloned.1.call-done = bf16[8,8,64,256]{3,2,0,1:T(8,128)(2,1)} async-done(((bf16[1,8,64,256]{3,2,0,1:T(8,128)(2,1)}), bf16[8,8,64,256]{3,2,0,1:T(8,128)(2,1)}) %all-gather.2.cloned.1.call-update) | async-done | bytes 2097168 | tf_op jit(solution)/shard_map/all_gather | solution.py:16
  165.2 12.0 %all-to-all-start.3 = ((bf16[32,1,64,256]{3,2,1,0:T(8,128)(2,1)}), bf16[32,1,64,256]{3,2,1,0:T(8,128)(2,1)}, u32[]{:S(2)}, u32[]{:S(2)}) async-start(bf16[32,1,64,256]{3,2,1,0:T(8,128)(2,1)} %bitcast.81), calls=%async_computation.3 | async-start | bytes 2097152 | tf_op jit(solution)/shard_map/all_to_all | solution.py:76
  178.4 7.9 %fusion.31 = pred[1024,8192]{1,0:T(32,128)(4,1)} fusion(s32[]{:T(128)S(6)} %select_n.65, pred[2048,2048]{1,0:T(32,128)(4,1)S(1)} %broadcast_in_dim.87, pred[2048,4096]{1,0:T(8,128)(4,1)} %bitcast.76), kind=kLoop, calls=%fused_computation.19 | loop fusion | flops 16777216 | bytes 20971524 | tf_op jit(solution)/shard_map/concatenate | solution.py:30
  189.7 15.5 %all-to-all-done.3 = bf16[32,1,64,256]{3,2,1,0:T(8,128)(2,1)} async-done(((bf16[32,1,64,256]{3,2,1,0:T(8,128)(2,1)}), bf16[32,1,64,256]{3,2,1,0:T(8,128)(2,1)}, u32[]{:S(2)}, u32[]{:S(2)}) %all-to-all-start.3) | async-done | bytes 1048608 | tf_op jit(solution)/shard_map/all_to_all | solution.py:76
  205.2 3.8 %maximum_bitcast_fusion = bf16[8192,256]{1,0:T(8,128)(2,1)} fusion(bf16[1,2048,256]{2,1,0:T(8,128)(2,1)} %bitcast.25, bf16[1,2048,256]{2,1,0:T(8,128)(2,1)} %bitcast.22, bf16[1,2048,256]{2,1,0:T(8,128)(2,1)} %bitcast.18, bf16[1,2048,256]{2,1,0:T(8,128)(2,1)} %slice.31), kind=kLoop, calls=%fused_computation.23 | loop fusion | flops 16777216 | bytes 8388608 | tf_op jit(solution)/shard_map/while/body/jit(dynamic_index_in_dim)/squeeze | solution.py:106
  209.0 54.6 %while.17 = (s32[]{:T(128)}, bf16[2,512,128]{2,1,0:T(8,128)(2,1)}, pred[2,512,8192]{2,1,0:T(32,128)(4,1)}, bf16[2,512,128]{2,1,0:T(8,128)(2,1)S(1)}, bf16[8192,256]{1,0:T(8,128)(2,1)}, /*index=5*/s32[]{:T(128)}) while((s32[]{:T(128)}, bf16[2,512,128]{2,1,0:T(8,128)(2,1)}, pred[2,512,8192]{2,1,0:T(32,128)(4,1)}, ...), condition=%wide.region_5.6_spmd, body=%wide.region_2.5_spmd.sunk | while | flops 2176973824 | bytes 58994244 | solution.py:104
  209.0 9.8 %fusion.56 = (f32[512]{0:T(512)S(1)}, f32[512,8192]{1,0:T(8,128)}) fusion(bf16[8192,256]{1,0:T(8,128)(2,1)} %get-tuple-element.118, bf16[2,512,128]{2,1,0:T(8,128)(2,1)S(1)} %get-tuple-element.117, s32[]{:T(128)} %get-tuple-element.108, pred[2,512,8192]{2,1,0:T(32,128)(4,1)} %get-tuple-element.116), kind=kOutput, calls=%fused_computation.45.clone.1 | convolution fusion | flops 1086324224 | bytes 23202816 | tf_op jit(solution)/shard_map/while/body/eval_jaxpr/while/body/eval_jaxpr/qd,kd->qk/dot_general | solution.py:34
  218.8 8.1 %fusion.57 = f32[512]{0:T(512)S(1)} fusion(f32[512,8192]{1,0:T(8,128)} %get-tuple-element.100, f32[512]{0:T(512)S(1)} %get-tuple-element.101), kind=kLoop, calls=%fused_computation.2.clone.1 | loop fusion | flops 8388096 | bytes 16781312 | tf_op jit(solution)/shard_map/while/body/eval_jaxpr/while/body/eval_jaxpr/reduce_sum | solution.py:40
  226.9 9.4 %fusion.58 = bf16[2,512,128]{2,1,0:T(8,128)(2,1)} fusion(bf16[2,512,128]{2,1,0:T(8,128)(2,1)} %get-tuple-element.109, s32[]{:T(128)} %get-tuple-element.108, bf16[8192,256]{1,0:T(8,128)(2,1)} %get-tuple-element.118, f32[512,8192]{1,0:T(8,128)} %get-tuple-element.100, f32[512]{0:T(512)S(1)} %get-tuple-element.101, f32[512]{0:T(512)S(1)} %fusion.57), kind=kOutput, calls=%fused_computation.11.clone.1 | convolution fusion | flops 1082261504 | bytes 19010048 | tf_op jit(solution)/shard_map/while/body/eval_jaxpr/while/body/eval_jaxpr/qk,kd->qd/dot_general | solution.py:42
  236.3 9.8 %fusion.56 = (f32[512]{0:T(512)S(1)}, f32[512,8192]{1,0:T(8,128)}) fusion(bf16[8192,256]{1,0:T(8,128)(2,1)} %get-tuple-element.118, bf16[2,512,128]{2,1,0:T(8,128)(2,1)S(1)} %get-tuple-element.117, s32[]{:T(128)} %get-tuple-element.108, pred[2,512,8192]{2,1,0:T(32,128)(4,1)} %get-tuple-element.116), kind=kOutput, calls=%fused_computation.45.clone.1 | convolution fusion | flops 1086324224 | bytes 23202816 | tf_op jit(solution)/shard_map/while/body/eval_jaxpr/while/body/eval_jaxpr/qd,kd->qk/dot_general | solution.py:34
  246.1 8.1 %fusion.57 = f32[512]{0:T(512)S(1)} fusion(f32[512,8192]{1,0:T(8,128)} %get-tuple-element.100, f32[512]{0:T(512)S(1)} %get-tuple-element.101), kind=kLoop, calls=%fused_computation.2.clone.1 | loop fusion | flops 8388096 | bytes 16781312 | tf_op jit(solution)/shard_map/while/body/eval_jaxpr/while/body/eval_jaxpr/reduce_sum | solution.py:40
  254.2 9.4 %fusion.58 = bf16[2,512,128]{2,1,0:T(8,128)(2,1)} fusion(bf16[2,512,128]{2,1,0:T(8,128)(2,1)} %get-tuple-element.109, s32[]{:T(128)} %get-tuple-element.108, bf16[8192,256]{1,0:T(8,128)(2,1)} %get-tuple-element.118, f32[512,8192]{1,0:T(8,128)} %get-tuple-element.100, f32[512]{0:T(512)S(1)} %get-tuple-element.101, f32[512]{0:T(512)S(1)} %fusion.57), kind=kOutput, calls=%fused_computation.11.clone.1 | convolution fusion | flops 1082261504 | bytes 19010048 | tf_op jit(solution)/shard_map/while/body/eval_jaxpr/while/body/eval_jaxpr/qk,kd->qd/dot_general | solution.py:42
  264.8 22.7 %all_to_all.20 = bf16[32,1,64,128]{3,2,1,0:T(8,128)(2,1)S(1)} all-to-all(bf16[32,1,64,128]{3,2,1,0:T(8,128)(2,1)S(1)} %broadcast_select_fusion), channel_id=1, replica_groups=mesh['view'=8,'tile'=32] {'tile'}, dimensions={0} | all-to-all | bytes 1048576 | tf_op jit(solution)/shard_map/all_to_all | solution.py:113
  (40 shorter events, 26.5 us)
Async XLA Ops:
  6.5 280.9 %copy-start = (bf16[1024,1536]{1,0:T(8,128)(2,1)S(1)}, bf16[1024,1536]{1,0:T(8,128)(2,1)}, u32[]{:S(2)}) copy-start(bf16[1024,1536]{1,0:T(8,128)(2,1)} %param.9) | copy-start | bytes 9437188
  6.5 9.8 %copy-start.3 = (bf16[2,64,1536]{2,1,0:T(8,128)(2,1)S(1)}, bf16[2,64,1536]{2,1,0:T(8,128)(2,1)}, u32[]{:S(2)}) copy-start(bf16[2,64,1536]{2,1,0:T(8,128)(2,1)} %param.7) | copy-start | bytes 1179652
  21.4 2.2 copy-start.1
  21.5 8.1 %collective-permute-start = (bf16[8,64,256]{2,1,0:T(8,128)(2,1)S(1)}, bf16[8,64,256]{2,1,0:T(8,128)(2,1)S(1)}, u32[]{:S(2)}, u32[]{:S(2)}) collective-permute-start(bf16[8,64,256]{2,1,0:T(8,128)(2,1)S(1)} %get-tuple-element.63), channel_id=1, source_target_pairs={{0,32},{32,64},{64,96},{96,128},{128,160},{160,192},{192,224},{224... | collective-permute-start | bytes 786440 | tf_op jit(solution)/shard_map/ppermute | solution.py:21
  29.7 88.9 %copy-start.2 = (s32[2,16,6]{1,0,2:T(2,128)S(1)}, s32[2,16,6]{1,0,2:T(2,128)}, u32[]{:S(2)}) copy-start(s32[2,16,6]{1,0,2:T(2,128)} %param.11) | copy-start | bytes 2308
  30.8 43.0 %all-to-all-start.1 = ((bf16[32,1,64,256]{3,2,1,0:T(8,128)(2,1)}), bf16[32,1,64,256]{3,2,1,0:T(8,128)(2,1)}, u32[]{:S(2)}, u32[]{:S(2)}) async-start(bf16[32,1,64,256]{3,2,1,0:T(8,128)(2,1)} %bitcast.83), calls=%async_computation.1 | async-start | bytes 2097152 | tf_op jit(solution)/shard_map/all_to_all | solution.py:77
  45.7 12.8 %collective-permute-start.1 = (bf16[8,64,256]{2,1,0:T(8,128)(2,1)}, bf16[8,64,256]{2,1,0:T(8,128)(2,1)S(1)}, u32[]{:S(2)}, u32[]{:S(2)}) collective-permute-start(bf16[8,64,256]{2,1,0:T(8,128)(2,1)} %get-tuple-element.66), channel_id=1, source_target_pairs={{0,224},{32,0},{64,32},{96,64},{128,96},{160,128},{192,160},{224,1... | collective-permute-start | bytes 786440 | tf_op jit(solution)/shard_map/ppermute | solution.py:21
  75.9 34.1 %all-to-all-start.2 = ((bf16[32,1,64,256]{3,2,1,0:T(8,128)(2,1)}), bf16[32,1,64,256]{3,2,1,0:T(8,128)(2,1)}, u32[]{:S(2)}, u32[]{:S(2)}) async-start(bf16[32,1,64,256]{3,2,1,0:T(8,128)(2,1)} %bitcast.82), calls=%async_computation.2 | async-start | bytes 2097152 | tf_op jit(solution)/shard_map/all_to_all | solution.py:78
  81.9 80.2 %all-gather.2.cloned.1.call-start = ((), (), s32[]{:S(2)}) async-start(), calls=%async_computation.5 | async-start | bytes 2359296 | tf_op jit(solution)/shard_map/all_gather | solution.py:16
  112.6 51.5 %all-to-all-start = ((bf16[32,1,64,384]{3,2,1,0:T(8,128)(2,1)}), bf16[32,1,64,384]{3,2,1,0:T(8,128)(2,1)}, u32[]{:S(2)}, u32[]{:S(2)}) async-start(bf16[32,1,64,384]{3,2,1,0:T(8,128)(2,1)} %bitcast.80), calls=%async_computation | async-start | bytes 3145728 | tf_op jit(solution)/shard_map/all_to_all | solution.py:75
  165.2 40.0 %all-to-all-start.3 = ((bf16[32,1,64,256]{3,2,1,0:T(8,128)(2,1)}), bf16[32,1,64,256]{3,2,1,0:T(8,128)(2,1)}, u32[]{:S(2)}, u32[]{:S(2)}) async-start(bf16[32,1,64,256]{3,2,1,0:T(8,128)(2,1)} %bitcast.81), calls=%async_computation.3 | async-start | bytes 2097152 | tf_op jit(solution)/shard_map/all_to_all | solution.py:76
Sparse Core Ops, SparseCore 0:
  86.3 75.7 all-gather.1
